TPU v7x, 256 devices: a whole 4x4x8 slice. The times are simulated.
256 devices in a mesh: band: 16 (over x, y_lo, core), dom: 16 (over z, y_hi).
Axes of the slice: x: 4, y: 4 (y_hi: 2, y_lo: 2; y = y_hi * 2 + y_lo), z: 8, core: 2. Of those that a mesh axis runs over, the one named last changes fastest.
Arguments:
- psi: float32 [1024, 64, 8, 128], P('band', 'dom'), may hold values from -6 to 6
- potential: float32 [64, 8, 128], P('dom'), may hold values from -1 to 1
- owner: int32 [1], replicated, may hold values from 0 to 15
Outputs:
- filtered: float32 [1024, 64, 8, 128], P('band', 'dom')
- intersection: float32 [64, 1024], P(None, 'band')
- hamiltonian: float32 [64, 1024], P(None, 'band')
Inputs may be any that keep to these rules, and one draw needn't show every extreme that they name: The owner's panel holds bands 64 * owner to 64 * owner + 63.
All inputs are finite; a program needn't handle non-finite values.
Results may differ from a plain program's by a relative error of at most 0.000084.
Values sent between devices are 32-bit elements; how exact they have to be, the bound alone decides.
No kernel may reach another device: no remote copies, remote signals or barrier semaphores. Data moves between devices by JAX's collectives and lax.ppermute only.
A program may use at most 64 MiB of HBM per device.

v0:
```python
import jax
import jax.numpy as jnp
from jax import lax
from jax.sharding import PartitionSpec as P

center = 4.9
halfwidth = 4.1


def extended_2(block, sides, width):
    for axis, dim in sides:
        count = lax.axis_size(axis)
        forward = [(i, i + 1) for i in range(count - 1)]
        forward.append((count - 1, 0))
        backward = [(target, source) for source, target in forward]
        low = lax.ppermute(
            lax.slice_in_dim(block, block.shape[dim] - width, None, axis=dim), axis, forward
        )
        high = lax.ppermute(lax.slice_in_dim(block, 0, width, axis=dim), axis, backward)
        block = jnp.concatenate([low, block, high], axis=dim)
    return block


def broadcast(array, axis, root):
    mine = lax.axis_index(axis) == root
    return lax.psum(jnp.where(mine, array, jnp.zeros_like(array)), axis)


def lap_periodic(grid_field, which_axis):
    outer = jnp.roll(grid_field, 2, which_axis) + jnp.roll(grid_field, -2, which_axis)
    nearer = jnp.roll(grid_field, 1, which_axis) + jnp.roll(grid_field, -1, which_axis)
    return -1.0 / 12.0 * outer + 4.0 / 3.0 * nearer - 2.5 * grid_field


def hamiltonian_apply(extended, local_potential):
    interior = extended[:, 2:-2]
    along_first = (
        -1.0 / 12.0 * (extended[:, :-4] + extended[:, 4:])
        + 4.0 / 3.0 * (extended[:, 1:-3] + extended[:, 3:-1])
        - 2.5 * interior
    )
    laplace = along_first + lap_periodic(interior, 2) + lap_periodic(interior, 3)
    return -0.5 * laplace + local_potential * interior


def shifted(extended, local_potential):
    return (hamiltonian_apply(extended, local_potential) - center * extended[:, 2:-2]) / halfwidth


def with_faces(grid_field):
    return extended_2(grid_field, (("dom", 1),), 2)


def body(psi, potential, owner):
    current = psi
    first_term = shifted(with_faces(current), potential)
    current = 2.0 * shifted(with_faces(first_term), potential) - current
    local_bands = current.shape[0]
    owner_root = owner[0]
    owned_panel = broadcast(current, "band", owner_root)
    total_cells = current.shape[1] * current.shape[2] * current.shape[3] * lax.axis_size("dom")
    scale = 1.0 / total_cells
    flattened = current.reshape(local_bands, -1)
    panel_flat = owned_panel.reshape(local_bands, -1)
    extended = extended_2(current, (("dom", 1),), 2)
    applied = hamiltonian_apply(extended, potential)
    ham_rows = jnp.einsum(
        "pc,bc->pb", panel_flat, applied.reshape(local_bands, -1), precision=lax.Precision.HIGHEST
    )
    over_rows = jnp.einsum("pc,bc->pb", panel_flat, flattened, precision=lax.Precision.HIGHEST)
    intersection, hamiltonian = lax.psum((over_rows * scale, ham_rows * scale), "dom")
    return (current, intersection, hamiltonian)


def solution(mesh):
    placed = (P("band", "dom", None, None), P("dom", None, None), P())
    return jax.shard_map(
        body,
        mesh=mesh,
        in_specs=placed,
        out_specs=(P("band", "dom", None, None), P(None, "band"), P(None, "band")),
        check_vma=False,
    )
```

profile of v0, /device:TPU:0, one launch (start us, length us, event | category | flops | bytes accessed | tf_op | source)
XLA Modules:
  0.0 314.2 jit_solution(11371170364938100870)
XLA Ops:
  9.5 6.8 %collective-permute-start.1 = (f32[64,2,8,128]{3,0,2,1:T(8,128)}, f32[64,2,8,128]{3,0,2,1:T(8,128)}, u32[]{:S(2)}, u32[]{:S(2)}) collective-permute-start(f32[64,2,8,128]{3,0,2,1:T(8,128)} %copy.37), channel_id=1, source_target_pairs={{1,0},{2,1},{3,2},{4,3},{5,4},{6,5},{7,6},{8,7},{9,8},{10,9},{11,1... | collective-permute-start | bytes 1572872 | tf_op jit(solution)/shard_map/ppermute | solution.py:19
  21.0 1.7 fusion.128
  22.8 1.6 fusion.124
  24.3 1.7 fusion.129
  26.0 1.7 fusion.130
  30.1 1.7 copy.41
  31.8 1.5 copy.43
  33.3 1.5 copy.46
  36.6 1.6 copy.47
  38.2 1.6 copy.50
  39.8 1.4 copy.39
  42.6 1.6 copy.52
  44.2 1.6 copy.53
  45.8 1.6 copy.51
  47.4 1.6 copy.54
  50.8 1.4 constant_dynamic-update-slice_fusion.2
  52.5 4.1 %broadcast_multiply_fusion = (f32[64,4,8,128]{3,0,2,1:T(8,128)S(1)}, f32[64,4,8,128]{3,0,2,1:T(8,128)S(1)}) fusion(f32[4,8,128]{2,1,0:T(8,128)} %param.4, f32[64,4,8,1]{3,0,2,1:T(8,128)S(1)} %copy-done.4, f32[64,4,8,127]{3,0,2,1:T(8,128)} %copy.54, f32[64,4,8,127]{3,0,2,1:T(8,128)S(1)} %copy-done.5, f32[64,4,8,1]{3,0,2,1:T(8,128)S(1)} %copy-done.3, ...), kind=kLoop, calls=%fused_computation.115 | loop fusion | flops 9175040 | bytes 15745024 | tf_op jit(solution)/shard_map/div | solution.py:47
  58.4 5.7 %collective-permute-start.3 = (f32[64,2,8,128]{3,0,2,1:T(8,128)S(1)}, f32[64,2,8,128]{3,0,2,1:T(8,128)S(1)}, u32[]{:S(2)}, u32[]{:S(2)}) collective-permute-start(f32[64,2,8,128]{3,0,2,1:T(8,128)S(1)} %get-tuple-element.31), channel_id=1, source_target_pairs={{1,0},{2,1},{3,2},{4,3},{5,4},{6,5},{7,6},{8,7},{9,8},{10,9},{11,1... | collective-permute-start | bytes 1572872 | tf_op jit(solution)/shard_map/ppermute | solution.py:19
  64.6 16.3 %collective-permute-done.2 = f32[64,2,8,128]{3,0,2,1:T(8,128)S(1)} collective-permute-done((f32[64,2,8,128]{3,0,2,1:T(8,128)S(1)}, f32[64,2,8,128]{3,0,2,1:T(8,128)S(1)}, u32[]{:S(2)}, u32[]{:S(2)}) %collective-permute-start.2) | collective-permute-done | bytes 524320 | tf_op jit(solution)/shard_map/ppermute | solution.py:16
  80.8 3.8 %collective-permute-done.3 = f32[64,2,8,128]{3,0,2,1:T(8,128)S(1)} collective-permute-done((f32[64,2,8,128]{3,0,2,1:T(8,128)S(1)}, f32[64,2,8,128]{3,0,2,1:T(8,128)S(1)}, u32[]{:S(2)}, u32[]{:S(2)}) %collective-permute-start.3) | collective-permute-done | bytes 524320 | tf_op jit(solution)/shard_map/ppermute | solution.py:19
  84.6 3.6 %broadcast_select_fusion = (f32[64,4,8,128]{3,0,2,1:T(8,128)}, f32[64,4,8,128]{3,0,2,1:T(8,128)S(1)}) fusion(pred[]{:T(512)S(6)} %eq.3, f32[64,4,8,128]{3,2,1,0:T(8,128)S(1)} %copy-done, f32[64,4,8,128]{3,0,2,1:T(8,128)S(1)} %get-tuple-element.11, f32[4,8,128]{2,1,0:T(8,128)S(1)} %broadcast_multiply_fusion.1, f32[64,4,8,1]{3,0,2,1:T(8,128)S(1)} %get-tuple-element.45, ...), kind=kLoop, calls=%fused_computation.114 | loop fusion | flops 10747904 | bytes 14696449 | tf_op jit(solution)/shard_map/jit(_where)/select_n | solution.py:26
  89.3 1.4 fusion.108
  92.1 1.7 fusion.105
  93.8 1.7 fusion.107
  95.7 5.5 %collective-permute-start.5 = (f32[64,2,8,128]{3,0,2,1:T(8,128)}, f32[64,2,8,128]{3,0,2,1:T(8,128)}, u32[]{:S(2)}, u32[]{:S(2)}) collective-permute-start(f32[64,2,8,128]{3,0,2,1:T(8,128)} %get-tuple-element.29), channel_id=1, source_target_pairs={{1,0},{2,1},{3,2},{4,3},{5,4},{6,5},{7,6},{8,7},{9,8},{10,9},{11,1... | collective-permute-start | bytes 1572872 | tf_op jit(solution)/shard_map/ppermute | solution.py:19
  101.2 1.4 fusion.110
  102.6 1.7 fusion.104
  105.0 1.6 copy.30
  107.3 113.6 %all-reduce.3.cloned.1.call-done = f32[64,4,8,128]{3,0,2,1:T(8,128)} async-done(((f32[64,4,8,128]{3,0,2,1:T(8,128)}), f32[64,4,8,128]{3,0,2,1:T(8,128)}) %all-reduce.3.cloned.1.call-update) | async-done | bytes 1048592 | tf_op jit(solution)/shard_map/psum | solution.py:26
  220.9 2.3 fusion.1
  223.2 6.2 %fusion = f32[64,64]{1,0:T(8,128)S(1)} fusion(f32[64,4,8,128]{3,0,2,1:T(8,128)S(1)} %copy-done.16, f32[64,4,8,128]{3,0,2,1:T(8,128)S(1)} %get-tuple-element.9, f32[64,2,8,128]{3,0,2,1:T(8,128)} %collective-permute-done.5, f32[64,2,8,128]{3,0,2,1:T(8,128)} %collective-permute-done.4, f32[64,4,6,128]{3,0,2,1:T(8,128)} %get-tuple-element.25, ...), kind=kOutput, calls=%fused_computation.9 | convolution fusion | flops 210767872 | bytes 11567104 | tf_op jit(solution)/shard_map/pc,bc->pb/dot_general | solution.py:67
  229.5 77.9 %all-reduce = (f32[64,64]{1,0:T(8,128)}, f32[64,64]{1,0:T(8,128)}) all-reduce(f32[64,64]{1,0:T(8,128)S(1)} %fusion.1, f32[64,64]{1,0:T(8,128)S(1)} %fusion), channel_id=1, replica_groups=mesh['band'=16,'dom'=16] {'dom'}, use_global_device_ids=true, to_apply=%region_1.2 | all-reduce | flops 8192 | bytes 65536 | tf_op jit(solution)/shard_map/psum | solution.py:71
  (78 shorter events, 20.3 us)
Async XLA Ops:
  7.2 213.7 %all-reduce.3.cloned.1.call-start = ((), (), s32[]{:S(2)}) async-start(), calls=%async_computation | async-start | bytes 2097152 | tf_op jit(solution)/shard_map/psum | solution.py:26
  8.5 8.8 %copy-start = (f32[64,4,8,128]{3,2,1,0:T(8,128)S(1)}, f32[64,4,8,128]{3,2,1,0:T(8,128)}, u32[]{:S(2)}) copy-start(f32[64,4,8,128]{3,2,1,0:T(8,128)} %param.3) | copy-start | bytes 3145732
  9.5 41.3 %collective-permute-start.1 = (f32[64,2,8,128]{3,0,2,1:T(8,128)}, f32[64,2,8,128]{3,0,2,1:T(8,128)}, u32[]{:S(2)}, u32[]{:S(2)}) collective-permute-start(f32[64,2,8,128]{3,0,2,1:T(8,128)} %copy.37), channel_id=1, source_target_pairs={{1,0},{2,1},{3,2},{4,3},{5,4},{6,5},{7,6},{8,7},{9,8},{10,9},{11,1... | collective-permute-start | bytes 1572872 | tf_op jit(solution)/shard_map/ppermute | solution.py:19
  17.3 31.7 %collective-permute-start = (f32[64,2,8,128]{3,0,2,1:T(8,128)}, f32[64,2,8,128]{3,0,2,1:T(8,128)}, u32[]{:S(2)}, u32[]{:S(2)}) collective-permute-start(f32[64,2,8,128]{3,0,2,1:T(8,128)} %copy.38), channel_id=1, source_target_pairs={{0,1},{1,2},{2,3},{3,4},{4,5},{5,6},{6,7},{7,8},{8,9},{9,10},{10,1... | collective-permute-start | bytes 1572872 | tf_op jit(solution)/shard_map/ppermute | solution.py:16
  26.0 1.7 copy-start.18
  27.7 4.2 %copy-start.15 = (f32[64,4,7,128]{3,2,1,0:T(8,128)S(1)}, f32[64,4,7,128]{3,2,1,0:T(8,128)}, u32[]{:S(2)}) copy-start(f32[64,4,7,128]{3,2,1,0:T(8,128)} %get-tuple-element.58) | copy-start | bytes 2752516
  33.3 2.1 copy-start.14
  35.4 1.2 copy-start.13
  36.0 2.2 copy-start.12
  38.2 1.6 copy-start.7
  38.2 3.0 copy-start.6
  39.8 2.8 copy-start.11
  41.3 2.9 copy-start.10
  44.2 1.6 copy-start.9
  45.8 1.6 copy-start.8
  49.0 3.3 %copy-start.5 = (f32[64,4,8,127]{3,0,2,1:T(8,128)S(1)}, f32[64,4,8,127]{3,0,2,1:T(8,128)}, u32[]{:S(2)}) copy-start(f32[64,4,8,127]{3,0,2,1:T(8,128)} %copy.51) | copy-start | bytes 3121156
  50.1 2.1 copy-start.1
  50.1 2.1 copy-start.2
  50.2 2.1 copy-start.3
  50.2 2.3 copy-start.4
  58.4 22.5 %collective-permute-start.2 = (f32[64,2,8,128]{3,0,2,1:T(8,128)S(1)}, f32[64,2,8,128]{3,0,2,1:T(8,128)S(1)}, u32[]{:S(2)}, u32[]{:S(2)}) collective-permute-start(f32[64,2,8,128]{3,0,2,1:T(8,128)S(1)} %get-tuple-element.30), channel_id=1, source_target_pairs={{0,1},{1,2},{2,3},{3,4},{4,5},{5,6},{6,7},{7,8},{8,9},{9,10},{10,1... | collective-permute-start | bytes 1572872 | tf_op jit(solution)/shard_map/ppermute | solution.py:16
  58.4 26.2 %collective-permute-start.3 = (f32[64,2,8,128]{3,0,2,1:T(8,128)S(1)}, f32[64,2,8,128]{3,0,2,1:T(8,128)S(1)}, u32[]{:S(2)}, u32[]{:S(2)}) collective-permute-start(f32[64,2,8,128]{3,0,2,1:T(8,128)S(1)} %get-tuple-element.31), channel_id=1, source_target_pairs={{1,0},{2,1},{3,2},{4,3},{5,4},{6,5},{7,6},{8,7},{9,8},{10,9},{11,1... | collective-permute-start | bytes 1572872 | tf_op jit(solution)/shard_map/ppermute | solution.py:19
  95.5 127.7 %collective-permute-start.4 = (f32[64,2,8,128]{3,0,2,1:T(8,128)}, f32[64,2,8,128]{3,0,2,1:T(8,128)}, u32[]{:S(2)}, u32[]{:S(2)}) collective-permute-start(f32[64,2,8,128]{3,0,2,1:T(8,128)} %get-tuple-element.28), channel_id=1, source_target_pairs={{0,1},{1,2},{2,3},{3,4},{4,5},{5,6},{6,7},{7,8},{8,9},{9,10},{10,1... | collective-permute-start | bytes 1572872 | tf_op jit(solution)/shard_map/ppermute | solution.py:16
  95.7 127.5 %collective-permute-start.5 = (f32[64,2,8,128]{3,0,2,1:T(8,128)}, f32[64,2,8,128]{3,0,2,1:T(8,128)}, u32[]{:S(2)}, u32[]{:S(2)}) collective-permute-start(f32[64,2,8,128]{3,0,2,1:T(8,128)} %get-tuple-element.29), channel_id=1, source_target_pairs={{1,0},{2,1},{3,2},{4,3},{5,4},{6,5},{7,6},{8,7},{9,8},{10,9},{11,1... | collective-permute-start | bytes 1572872 | tf_op jit(solution)/shard_map/ppermute | solution.py:19
  106.6 116.7 %copy-start.19 = (f32[4,8,128]{2,1,0:T(8,128)S(1)}, f32[4,8,128]{2,1,0:T(8,128)}, u32[]{:S(2)}) copy-start(f32[4,8,128]{2,1,0:T(8,128)} %param.4) | copy-start | bytes 49156
  220.9 2.3 copy-start.16
  220.9 2.4 copy-start.17
Sparse Core Ops, SparseCore 0:
  95.6 125.2 all-reduce.2
where the time goes:
time: 315 us; the launch traced here: 314 us
  waiting for transfers between devices  134 us (43%)
  blocking collectives  77.9 us (25%)
  local copies, waits for them, and re-layouts  53 us (17%)
  starting transfers between devices  18.3 us (6%)
  between operations  15.1 us (5%)
  matrix products  8.52 us (3%)
  other arithmetic  7.73 us (2%)
    psum x1, waiting for transfers between devices, broadcast(): return lax.psum(jnp.where(mine, array, jnp.zeros_like(array)), axis)  114 us
    psum x1, blocking collectives, body(): lax.psum((over_rows * scale, ham_rows * scale), 'dom')  77.9 us
    unnamed x60, local copies, waits for them, and re-layouts  25.5 us
    ppermute x3, starting transfers between devices, extended_2(): lax.ppermute(lax.slice_in_dim(block, 0, width, axis=dim), axis, backward)  18 us
    ppermute x3, waiting for transfers between devices, extended_2(): lax.ppermute(lax.slice_in_dim(block, block.shape[dim] - width, None, axis...  16.3 us
    slice x8, local copies, waits for them, and re-layouts, lap_periodic(): jnp.roll(grid_field, 2, which_axis) + jnp.roll(grid_field, -2, which_axis)  6.59 us
  transfers between devices with their start and end apart: 7, of which 3 were waited for; matrix products, arithmetic and copies ran while one was open for 13% of the time, Pallas kernels for 0%

commit v1 on v0

--- a/solution.py
+++ b/solution.py
@@ -23,7 +23,7 @@
 
 def broadcast(array, axis, root):
     mine = lax.axis_index(axis) == root
-    return lax.psum(jnp.where(mine, array, jnp.zeros_like(array)), axis)
+    return jnp.sum(lax.all_gather(jnp.where(mine, array, jnp.zeros_like(array)), axis), axis=0)
 
 
 def lap_periodic(grid_field, which_axis):

time: 315 us -> 281 us (0.89)
  local copies, waits for them, and re-layouts: 53 us -> 18.8 us
  waiting for transfers between devices: 134 us -> 120 us
  other arithmetic: 7.73 us -> 18.5 us
  blocking collectives: 77.9 us -> 82.2 us
  matrix products: 8.52 us -> 4.28 us
    psum x1 -> x0, waiting for transfers between devices: 114 us -> none  [broadcast(): return lax.psum(jnp.where(mine, array, jnp.zeros_like(array)), axis)]
    all_gather x0 -> x1, waiting for transfers between devices: none -> 63.4 us  [broadcast(): lax.all_gather(jnp.where(mine, array, jnp.zeros_like(array)), axis)]
    ppermute x3, waiting for transfers between devices: 16.3 us -> 43.1 us  [extended_2(): lax.ppermute(lax.slice_in_dim(block, block.shape[dim] - width, None, axis...]
    unnamed x60 -> x17, local copies, waits for them, and re-layouts: 25.5 us -> 0.07 us
    ppermute x3, waiting for transfers between devices: 3.82 us -> 13.4 us  [extended_2(): lax.ppermute(lax.slice_in_dim(block, 0, width, axis=dim), axis, backward)]
    reduce_sum x0 -> x1, other arithmetic: none -> 7.91 us  [broadcast(): jnp.sum(lax.all_gather(jnp.where(mine, array, jnp.zeros_like(array)), axi...]
    slice x4, local copies, waits for them, and re-layouts: 5.53 us -> 1.15 us  [lap_periodic(): jnp.roll(grid_field, -1, which_axis)]
    psum x1, blocking collectives: 77.9 us -> 82.2 us  [body(): lax.psum((over_rows * scale, ham_rows * scale), 'dom')]
  transfers between devices with their start and end apart: 7 -> 7, of which waited for: 3 -> 7; matrix products, arithmetic and copies ran while one was open for 13% -> 6% of each run, Pallas kernels for 0% -> 0%
where the time goes in v1:
time: 281 us; the launch traced here: 280 us
  waiting for transfers between devices  120 us (43%)
  blocking collectives  82.2 us (29%)
  starting transfers between devices  20.9 us (7%)
  local copies, waits for them, and re-layouts  18.8 us (7%)
  other arithmetic  18.5 us (7%)
  between operations  15 us (5%)
  matrix products  4.28 us (2%)
    psum x1, blocking collectives, body(): lax.psum((over_rows * scale, ham_rows * scale), 'dom')  82.2 us
    all_gather x1, waiting for transfers between devices, broadcast(): lax.all_gather(jnp.where(mine, array, jnp.zeros_like(array)), axis)  63.4 us
    ppermute x3, waiting for transfers between devices, extended_2(): lax.ppermute(lax.slice_in_dim(block, block.shape[dim] - width, None, axis...  43.1 us
    ppermute x3, starting transfers between devices, extended_2(): lax.ppermute(lax.slice_in_dim(block, 0, width, axis=dim), axis, backward)  16.2 us
    ppermute x3, waiting for transfers between devices, extended_2(): lax.ppermute(lax.slice_in_dim(block, 0, width, axis=dim), axis, backward)  13.4 us
    reduce_sum x1, other arithmetic, broadcast(): jnp.sum(lax.all_gather(jnp.where(mine, array, jnp.zeros_like(array)), axi...  7.91 us
    slice x8, local copies, waits for them, and re-layouts, lap_periodic(): jnp.roll(grid_field, 1, which_axis) + jnp.roll(grid_field, -1, which_axis)  7.03 us
    slice x8, local copies, waits for them, and re-layouts, lap_periodic(): jnp.roll(grid_field, 2, which_axis) + jnp.roll(grid_field, -2, which_axis)  6.73 us
  transfers between devices with their start and end apart: 7, of which 7 were waited for; matrix products, arithmetic and copies ran while one was open for 6% of the time, Pallas kernels for 0%

profile of v1, /device:TPU:0, one launch (start us, length us, event | category | flops | bytes accessed | tf_op | source)
XLA Modules:
  0.0 279.5 jit_solution(364802518205164511)
XLA Ops:
  7.2 2.3 fusion.85
  9.6 1.5 collective-permute-start
  11.0 5.3 %collective-permute-start.1 = (f32[64,2,8,128]{3,2,1,0:T(8,128)}, f32[64,2,8,128]{3,2,1,0:T(8,128)S(1)}, u32[]{:S(2)}, u32[]{:S(2)}) collective-permute-start(f32[64,2,8,128]{3,2,1,0:T(8,128)} %get-tuple-element.48), channel_id=1, source_target_pairs={{1,0},{2,1},{3,2},{4,3},{5,4},{6,5},{7,6},{8,7},{9,8},{10,9},{11,1... | collective-permute-start | bytes 1572872 | tf_op jit(solution)/shard_map/ppermute | solution.py:19
  16.3 1.4 fusion.91
  17.7 1.7 fusion.90
  19.4 1.6 fusion.87
  21.1 1.7 fusion.93
  22.8 1.7 fusion.92
  24.5 1.7 fusion.89
  26.2 0.9 fusion.86
  27.0 0.8 fusion.88
  28.5 5.3 %collective-permute-done = f32[64,2,8,128]{3,2,1,0:T(8,128)S(1)} collective-permute-done((f32[64,2,8,128]{3,2,1,0:T(8,128)}, f32[64,2,8,128]{3,2,1,0:T(8,128)S(1)}, u32[]{:S(2)}, u32[]{:S(2)}) %collective-permute-start) | collective-permute-done | bytes 524320 | tf_op jit(solution)/shard_map/ppermute | solution.py:16
  34.0 3.4 %collective-permute-done.1 = f32[64,2,8,128]{3,2,1,0:T(8,128)S(1)} collective-permute-done((f32[64,2,8,128]{3,2,1,0:T(8,128)}, f32[64,2,8,128]{3,2,1,0:T(8,128)S(1)}, u32[]{:S(2)}, u32[]{:S(2)}) %collective-permute-start.1) | collective-permute-done | bytes 524320 | tf_op jit(solution)/shard_map/ppermute | solution.py:19
  37.5 4.6 %broadcast_multiply_fusion = (f32[64,4,8,128]{3,2,1,0:T(8,128)S(1)}, f32[64,4,8,128]{3,2,1,0:T(8,128)S(1)}) fusion(f32[64,4,8,128]{3,2,1,0:T(8,128)S(1)} %copy-done, f32[4,8,128]{2,1,0:T(8,128)S(1)} %copy-done.7, f32[64,4,8,1]{3,2,1,0:T(8,128)} %get-tuple-element.62, f32[64,4,8,127]{3,2,1,0:T(8,128)} %get-tuple-element.64, ...), kind=kLoop, calls=%fused_computation.95 | loop fusion | flops 9175040 | bytes 15745024 | tf_op jit(solution)/shard_map/div | solution.py:47
  44.0 2.7 collective-permute-start.2
  46.7 5.4 %collective-permute-start.3 = (f32[64,2,8,128]{3,2,1,0:T(8,128)S(1)}, f32[64,2,8,128]{3,2,1,0:T(8,128)S(1)}, u32[]{:S(2)}, u32[]{:S(2)}) collective-permute-start(f32[64,2,8,128]{3,2,1,0:T(8,128)S(1)} %get-tuple-element.28), channel_id=1, source_target_pairs={{1,0},{2,1},{3,2},{4,3},{5,4},{6,5},{7,6},{8,7},{9,8},{10,9},{11,1... | collective-permute-start | bytes 1572872 | tf_op jit(solution)/shard_map/ppermute | solution.py:19
  52.6 15.7 %collective-permute-done.2 = f32[64,2,8,128]{3,2,1,0:T(8,128)S(1)} collective-permute-done((f32[64,2,8,128]{3,2,1,0:T(8,128)S(1)}, f32[64,2,8,128]{3,2,1,0:T(8,128)S(1)}, u32[]{:S(2)}, u32[]{:S(2)}) %collective-permute-start.2) | collective-permute-done | bytes 524320 | tf_op jit(solution)/shard_map/ppermute | solution.py:16
  68.3 3.7 %collective-permute-done.3 = f32[64,2,8,128]{3,2,1,0:T(8,128)S(1)} collective-permute-done((f32[64,2,8,128]{3,2,1,0:T(8,128)S(1)}, f32[64,2,8,128]{3,2,1,0:T(8,128)S(1)}, u32[]{:S(2)}, u32[]{:S(2)}) %collective-permute-start.3) | collective-permute-done | bytes 524320 | tf_op jit(solution)/shard_map/ppermute | solution.py:19
  72.0 3.5 %broadcast_select_fusion = (f32[64,4,8,128]{3,2,1,0:T(8,128)}, f32[64,4,8,128]{3,2,1,0:T(8,128)S(1)}) fusion(pred[]{:T(512)S(6)} %eq.3, f32[64,4,8,128]{3,2,1,0:T(8,128)S(1)} %copy-done, f32[64,4,8,128]{3,2,1,0:T(8,128)S(1)} %get-tuple-element.8, f32[4,8,128]{2,1,0:T(8,128)S(1)} %broadcast_multiply_fusion.1, f32[64,4,8,1]{3,2,1,0:T(8,128)S(1)} %get-tuple-element.42, ...), kind=kLoop, calls=%fused_computation.94 | loop fusion | flops 10747904 | bytes 14696449 | tf_op jit(solution)/shard_map/jit(_where)/select_n | solution.py:26
  75.9 5.6 %collective-permute-start.5 = (f32[64,2,8,128]{3,2,1,0:T(8,128)S(1)}, f32[64,2,8,128]{3,2,1,0:T(8,128)S(1)}, u32[]{:S(2)}, u32[]{:S(2)}) collective-permute-start(f32[64,2,8,128]{3,2,1,0:T(8,128)S(1)} %get-tuple-element.26), channel_id=1, source_target_pairs={{1,0},{2,1},{3,2},{4,3},{5,4},{6,5},{7,6},{8,7},{9,8},{10,9},{11,1... | collective-permute-start | bytes 1572872 | tf_op jit(solution)/shard_map/ppermute | solution.py:19
  81.6 0.4 fusion.69
  82.5 0.4 fusion.68
  82.9 0.4 fusion.70
  83.4 0.4 fusion.67
  83.8 22.2 %collective-permute-done.4 = f32[64,2,8,128]{3,2,1,0:T(8,128)S(1)} collective-permute-done((f32[64,2,8,128]{3,2,1,0:T(8,128)S(1)}, f32[64,2,8,128]{3,2,1,0:T(8,128)S(1)}, u32[]{:S(2)}, u32[]{:S(2)}) %collective-permute-start.4) | collective-permute-done | bytes 524320 | tf_op jit(solution)/shard_map/ppermute | solution.py:16
  106.0 6.3 %collective-permute-done.5 = f32[64,2,8,128]{3,2,1,0:T(8,128)S(1)} collective-permute-done((f32[64,2,8,128]{3,2,1,0:T(8,128)S(1)}, f32[64,2,8,128]{3,2,1,0:T(8,128)S(1)}, u32[]{:S(2)}, u32[]{:S(2)}) %collective-permute-start.5) | collective-permute-done | bytes 524320 | tf_op jit(solution)/shard_map/ppermute | solution.py:19
  112.3 2.5 fusion.10
  114.9 63.4 %all-gather.3.cloned.1.call-done = f32[1024,4,8,128]{3,2,1,0:T(8,128)} async-done(((f32[64,4,8,128]{3,2,1,0:T(8,128)}), f32[1024,4,8,128]{3,2,1,0:T(8,128)}) %all-gather.3.cloned.1.call-update) | async-done | bytes 16777232 | tf_op jit(solution)/shard_map/all_gather | solution.py:26
  178.3 7.9 %reduce_sum.9 = f32[64,4,8,128]{3,2,1,0:T(8,128)S(1)} reduce(f32[16,64,4,8,128]{4,3,2,1,0:T(8,128)} %bitcast.15, f32[]{:T(128)} %constant.29.clone.1), dimensions={0}, to_apply=%region_0.1 | reduce | flops 3932160 | bytes 17825796 | tf_op jit(solution)/shard_map/reduce_sum | solution.py:26
  186.2 2.1 fusion.1
  188.3 2.1 fusion
  190.5 82.2 %all-reduce = (f32[64,64]{1,0:T(8,128)}, f32[64,64]{1,0:T(8,128)}) all-reduce(f32[64,64]{1,0:T(8,128)S(1)} %fusion.1, f32[64,64]{1,0:T(8,128)S(1)} %fusion), channel_id=1, replica_groups=mesh['band'=16,'dom'=16] {'dom'}, use_global_device_ids=true, to_apply=%region_1.2 | all-reduce | flops 8192 | bytes 65536 | tf_op jit(solution)/shard_map/psum | solution.py:71
  (37 shorter events, 3.9 us)
Async XLA Ops:
  7.2 9.2 %copy-start = (f32[64,4,8,128]{3,2,1,0:T(8,128)S(1)}, f32[64,4,8,128]{3,2,1,0:T(8,128)}, u32[]{:S(2)}) copy-start(f32[64,4,8,128]{3,2,1,0:T(8,128)} %param.3) | copy-start | bytes 3145732
  7.2 171.1 %all-gather.3.cloned.1.call-start = ((), (), s32[]{:S(2)}) async-start(), calls=%async_computation | async-start | bytes 17825792 | tf_op jit(solution)/shard_map/all_gather | solution.py:26
  9.6 24.2 %collective-permute-start = (f32[64,2,8,128]{3,2,1,0:T(8,128)}, f32[64,2,8,128]{3,2,1,0:T(8,128)S(1)}, u32[]{:S(2)}, u32[]{:S(2)}) collective-permute-start(f32[64,2,8,128]{3,2,1,0:T(8,128)} %get-tuple-element.47), channel_id=1, source_target_pairs={{0,1},{1,2},{2,3},{3,4},{4,5},{5,6},{6,7},{7,8},{8,9},{9,10},{10,1... | collective-permute-start | bytes 1572872 | tf_op jit(solution)/shard_map/ppermute | solution.py:16
  11.0 26.3 %collective-permute-start.1 = (f32[64,2,8,128]{3,2,1,0:T(8,128)}, f32[64,2,8,128]{3,2,1,0:T(8,128)S(1)}, u32[]{:S(2)}, u32[]{:S(2)}) collective-permute-start(f32[64,2,8,128]{3,2,1,0:T(8,128)} %get-tuple-element.48), channel_id=1, source_target_pairs={{1,0},{2,1},{3,2},{4,3},{5,4},{6,5},{7,6},{8,7},{9,8},{10,9},{11,1... | collective-permute-start | bytes 1572872 | tf_op jit(solution)/shard_map/ppermute | solution.py:19
  26.2 2.3 copy-start.7
  33.8 3.6 %copy-start.6 = (f32[64,4,6,128]{3,2,1,0:T(8,128)S(1)}, f32[64,4,6,128]{3,2,1,0:T(8,128)}, u32[]{:S(2)}) copy-start(f32[64,4,6,128]{3,2,1,0:T(8,128)} %get-tuple-element.52) | copy-start | bytes 2359300
  33.8 3.6 %copy-start.2 = (f32[64,4,8,126]{3,2,1,0:T(8,128)S(1)}, f32[64,4,8,126]{3,2,1,0:T(8,128)}, u32[]{:S(2)}) copy-start(f32[64,4,8,126]{3,2,1,0:T(8,128)} %get-tuple-element.60) | copy-start | bytes 3096580
  33.8 3.6 %copy-start.3 = (f32[64,4,8,2]{3,2,1,0:T(8,128)S(1)}, f32[64,4,8,2]{3,2,1,0:T(8,128)}, u32[]{:S(2)}) copy-start(f32[64,4,8,2]{3,2,1,0:T(8,128)} %get-tuple-element.57) | copy-start | bytes 49156
  33.8 3.6 %copy-start.4 = (f32[64,4,8,2]{3,2,1,0:T(8,128)S(1)}, f32[64,4,8,2]{3,2,1,0:T(8,128)}, u32[]{:S(2)}) copy-start(f32[64,4,8,2]{3,2,1,0:T(8,128)} %get-tuple-element.58) | copy-start | bytes 49156
  33.8 3.6 %copy-start.5 = (f32[64,4,6,128]{3,2,1,0:T(8,128)S(1)}, f32[64,4,6,128]{3,2,1,0:T(8,128)}, u32[]{:S(2)}) copy-start(f32[64,4,6,128]{3,2,1,0:T(8,128)} %get-tuple-element.51) | copy-start | bytes 2359300
  44.0 24.3 %collective-permute-start.2 = (f32[64,2,8,128]{3,2,1,0:T(8,128)S(1)}, f32[64,2,8,128]{3,2,1,0:T(8,128)S(1)}, u32[]{:S(2)}, u32[]{:S(2)}) collective-permute-start(f32[64,2,8,128]{3,2,1,0:T(8,128)S(1)} %get-tuple-element.27), channel_id=1, source_target_pairs={{0,1},{1,2},{2,3},{3,4},{4,5},{5,6},{6,7},{7,8},{8,9},{9,10},{10,1... | collective-permute-start | bytes 1572872 | tf_op jit(solution)/shard_map/ppermute | solution.py:16
  46.7 25.3 %collective-permute-start.3 = (f32[64,2,8,128]{3,2,1,0:T(8,128)S(1)}, f32[64,2,8,128]{3,2,1,0:T(8,128)S(1)}, u32[]{:S(2)}, u32[]{:S(2)}) collective-permute-start(f32[64,2,8,128]{3,2,1,0:T(8,128)S(1)} %get-tuple-element.28), channel_id=1, source_target_pairs={{1,0},{2,1},{3,2},{4,3},{5,4},{6,5},{7,6},{8,7},{9,8},{10,9},{11,1... | collective-permute-start | bytes 1572872 | tf_op jit(solution)/shard_map/ppermute | solution.py:19
  75.5 110.7 %copy-start.1 = (f32[64,4,8,128]{3,2,1,0:T(8,128)}, f32[64,4,8,128]{3,2,1,0:T(8,128)S(1)}, u32[]{:S(2)}) copy-start(f32[64,4,8,128]{3,2,1,0:T(8,128)S(1)} %get-tuple-element.6) | copy-start | bytes 3145732
  75.6 30.4 %collective-permute-start.4 = (f32[64,2,8,128]{3,2,1,0:T(8,128)S(1)}, f32[64,2,8,128]{3,2,1,0:T(8,128)S(1)}, u32[]{:S(2)}, u32[]{:S(2)}) collective-permute-start(f32[64,2,8,128]{3,2,1,0:T(8,128)S(1)} %get-tuple-element.25), channel_id=1, source_target_pairs={{0,1},{1,2},{2,3},{3,4},{4,5},{5,6},{6,7},{7,8},{8,9},{9,10},{10,1... | collective-permute-start | bytes 1572872 | tf_op jit(solution)/shard_map/ppermute | solution.py:16
  75.9 36.4 %collective-permute-start.5 = (f32[64,2,8,128]{3,2,1,0:T(8,128)S(1)}, f32[64,2,8,128]{3,2,1,0:T(8,128)S(1)}, u32[]{:S(2)}, u32[]{:S(2)}) collective-permute-start(f32[64,2,8,128]{3,2,1,0:T(8,128)S(1)} %get-tuple-element.26), channel_id=1, source_target_pairs={{1,0},{2,1},{3,2},{4,3},{5,4},{6,5},{7,6},{8,7},{9,8},{10,9},{11,1... | collective-permute-start | bytes 1572872 | tf_op jit(solution)/shard_map/ppermute | solution.py:19
Sparse Core Ops, SparseCore 0:
  75.6 102.6 all-gather.2
